TPU v7x, 256 devices: a whole 4x4x8 slice. The times are simulated.
256 devices in a mesh: dp: 32 (over x, z), tensor: 8 (over y, core).
Axes of the slice: x: 4, y: 4, z: 8, core: 2. Of those that a mesh axis runs over, the one named last changes fastest.
Arguments:
- counts: int32 [32], replicated, may hold values from 1 to 32, 512 in all
- keys: bfloat16 [1024, 28672], P('dp'), may hold values from -6 to 6
- inverse_cov: bfloat16 [28672, 28672], P('tensor', 'dp'), as said below
- hidden: bfloat16 [1024, 8192], P('dp', 'tensor'), may hold values from -6 to 6
- targets: bfloat16 [1024, 8192], P('dp', 'tensor'), may hold values from -48 to 48
- down_weight: bfloat16 [8192, 28672], P('tensor', 'dp'), may hold values from -0.03125 to 0.03125
Outputs:
- new_weight: bfloat16 [8192, 28672], P('tensor', 'dp')
- next_resid: bfloat16 [1024, 8192], P('dp', 'tensor')
Inputs may be any that keep to these rules, and one draw needn't show every extreme that they name: Group g has counts[g] live edits in its first counts[g] slots; the counts sum to 512; some group holds 32. `inverse_cov`: symmetric positive definite.
All inputs are finite; a program needn't handle non-finite values.
Results may differ from a plain program's by a relative error of at most 0.01.
The roundings to bfloat16 on the way count: a program that leaves them out, or rounds other values in their place, can miss the bound.
Values may be sent and summed in bfloat16 or wider, within the bound.
No kernel may reach another device: no remote copies, remote signals or barrier semaphores. Data moves between devices by JAX's collectives and lax.ppermute only.
A program may use at most 128 MiB of HBM per device.

v0:
```python
import jax
import jax.numpy as jnp
from jax import lax
from jax.sharding import PartitionSpec as P

LAYERS_LEFT = 3


def cholesky_solve(system, right_side):
    factor = jnp.linalg.cholesky(system)
    middle = lax.linalg.triangular_solve(factor, right_side, left_side=True, lower=True)
    return lax.linalg.triangular_solve(factor, middle, left_side=True, lower=True, transpose_a=True)


def rows_product(left, right):
    return lax.dot_general(
        left, right, (((1,), (1,)), ((), ())), preferred_element_type=jnp.float32
    )


def pick(select, values):
    return jnp.dot(select, values, preferred_element_type=jnp.float32).astype(values.dtype)


def gather_rows(x, axis):
    n = lax.axis_size(axis)
    copies = jnp.broadcast_to(x[None], (n,) + x.shape)
    return lax.all_to_all(copies, axis, 0, 0, tiled=True).reshape((n * x.shape[0],) + x.shape[1:])


def scatter_rows_sum(x, axis):
    n = lax.axis_size(axis)
    parts = lax.all_to_all(x.reshape((n, x.shape[0] // n) + x.shape[1:]), axis, 0, 0, tiled=True)
    return parts.sum(0)


def per_device(counts, keys, inverse_cov, hidden, targets, down_weight):
    slot_count = keys.shape[0]
    group_size = lax.axis_size("dp")
    group_index = lax.axis_index("dp")
    tensor_index = lax.axis_index("tensor")
    width_part = inverse_cov.shape[0]
    row_total = slot_count * group_size
    live_total = row_total // 2
    ends = jnp.cumsum(counts)
    starts = ends - counts
    compact = jnp.arange(live_total, dtype=jnp.int32)
    owner = jnp.minimum(jnp.sum(compact[:, None] >= ends[None, :], axis=1), group_size - 1)
    row_of = owner * slot_count + compact - starts[owner]
    select = (row_of[:, None] == jnp.arange(row_total, dtype=jnp.int32)[None, :]).astype(
        jnp.bfloat16
    )
    slots = jnp.arange(slot_count, dtype=jnp.int32)
    live_vec = slots < counts[group_index]
    live_slot = live_vec[:, None]
    own_compact = jnp.where(live_vec, starts[group_index] + slots, 0)
    masked_keys = jnp.where(live_slot, keys, jnp.zeros_like(keys))
    column_part = lax.dynamic_slice_in_dim(masked_keys, tensor_index * width_part, width_part, 1)
    columns = lax.all_to_all(masked_keys, "dp", split_axis=1, concat_axis=0, tiled=True)
    gathered = lax.all_gather(column_part, "dp", axis=0, tiled=True)
    change = (targets.astype(jnp.float32) - hidden.astype(jnp.float32)) / LAYERS_LEFT
    resid_local = jnp.where(live_slot, change, jnp.zeros_like(change)).astype(jnp.bfloat16)
    gathered, columns = lax.optimization_barrier((gathered, columns))
    resid_all = lax.all_gather(resid_local, "dp", axis=0, tiled=True)
    keys_c = pick(select, gathered)
    columns_c = pick(select, columns)
    partial_q = jnp.dot(keys_c, inverse_cov, preferred_element_type=jnp.float32)
    tensor_size = lax.axis_size("tensor")
    parts_q = (
        lax.all_to_all(
            partial_q.astype(jnp.bfloat16).reshape((tensor_size, -1) + partial_q.shape[1:]),
            "tensor",
            0,
            0,
            tiled=True,
        )
        .astype(jnp.float32)
        .sum(0)
    )
    precond_c = gather_rows(parts_q.astype(jnp.bfloat16), "tensor")
    gram_c = gather_rows(scatter_rows_sum(rows_product(precond_c, columns_c), "dp"), "dp")
    base_partial = rows_product(columns, down_weight)
    gram_c, base_partial = lax.optimization_barrier((gram_c, base_partial))
    base = scatter_rows_sum(base_partial, "dp")
    system = gram_c + jnp.eye(live_total, dtype=jnp.float32)
    factor = jnp.linalg.cholesky(system)
    factor, resid_all = lax.optimization_barrier((factor, resid_all))
    resid_c = pick(select, resid_all)
    middle = lax.linalg.triangular_solve(
        factor, resid_c.astype(jnp.float32), left_side=True, lower=True
    )
    solved_c = lax.linalg.triangular_solve(
        factor, middle, left_side=True, lower=True, transpose_a=True
    ).astype(jnp.bfloat16)
    weight_delta = lax.dot_general(
        solved_c, precond_c, (((0,), (0,)), ((), ())), preferred_element_type=jnp.float32
    )
    new_weight = (down_weight.astype(jnp.float32) + weight_delta).astype(jnp.bfloat16)
    gram_own = jnp.where(live_slot, jnp.take(gram_c, own_compact, axis=1).T, 0.0)
    extra = jnp.dot(
        gram_own,
        solved_c.astype(jnp.float32),
        precision=lax.Precision.HIGHEST,
        preferred_element_type=jnp.float32,
    )
    summed = hidden.astype(jnp.float32) + (base + extra)
    next_resid = jnp.where(live_slot, summed, jnp.zeros_like(summed)).astype(jnp.bfloat16)
    return (new_weight, next_resid)


def solution(mesh):
    in_specs = (
        P(),
        P("dp", None),
        P("tensor", "dp"),
        P("dp", "tensor"),
        P("dp", "tensor"),
        P("tensor", "dp"),
    )
    out_specs = (P("tensor", "dp"), P("dp", "tensor"))
    return jax.shard_map(
        per_device, mesh=mesh, in_specs=in_specs, out_specs=out_specs, check_vma=False
    )
```

profile of v0, /device:TPU:2, one launch (start us, length us, event | category | flops | bytes accessed | tf_op | source)
XLA Modules:
  0.0 408.6 jit_solution(1317642860902086746)
XLA Ops:
  12.9 11.7 %all-to-all-start = ((bf16[32,32,896]{2,0,1:T(8,128)(2,1)}), bf16[32,32,896]{2,0,1:T(8,128)(2,1)S(1)}, u32[]{:S(2)}, u32[]{:S(2)}) async-start(bf16[32,32,896]{2,0,1:T(8,128)(2,1)} %bitcast.127), calls=%async_computation | async-start | bytes 3670016 | tf_op jit(solution)/shard_map/all_to_all | solution.py:59
  26.4 4.4 %compare_select_fusion.1 = (s32[512,1]{0,1:T(1,128)S(1)}, s32[512,1]{0,1:T(1,128)S(1)}) fusion(s32[]{:T(128)} %bitcast.27, s32[]{:T(128)} %bitcast.28, s32[]{:T(128)} %bitcast.29, s32[]{:T(128)} %bitcast.30, s32[]{:T(128)} %bitcast.31, s32[]{:T(128)} %bitcast.33, s32[]{:T(128)} %bitcast.32, s32[512,1]{0,1:T(1,128)S(1)} %bitcast.136), kind=kLoop, calls=%fused_computation.136 | loop fusion | flops 7680 | bytes 6172 | tf_op jit(solution)/shard_map/gather | solution.py:49
  31.0 15.8 %select_subtract_fusion = s32[512]{0:T(512)S(1)} fusion(pred[512]{0:T(512)(128)(4,1)S(1)} %get-tuple-element.46, pred[512]{0:T(512)(128)(4,1)S(1)} %get-tuple-element.45, pred[512]{0:T(512)(128)(4,1)S(1)} %get-tuple-element.44, pred[512]{0:T(512)(128)(4,1)S(1)} %get-tuple-element.43, pred[512]{0:T(512)(128)(4,1)S(1)} %get-tuple-element.42, ...), kind=kLoop, calls=%fused_computation.145 | loop fusion | flops 14848 | bytes 19044 | tf_op jit(solution)/shard_map/sub | solution.py:49
  46.8 28.5 %all-to-all-done = bf16[32,32,896]{2,0,1:T(8,128)(2,1)S(1)} async-done(((bf16[32,32,896]{2,0,1:T(8,128)(2,1)}), bf16[32,32,896]{2,0,1:T(8,128)(2,1)S(1)}, u32[]{:S(2)}, u32[]{:S(2)}) %all-to-all-start) | async-done | bytes 1835040 | tf_op jit(solution)/shard_map/all_to_all | solution.py:59
  75.4 41.5 %all-gather.3.cloned.1.call-done = bf16[1024,3584]{1,0:T(8,128)(2,1)} async-done(((bf16[32,3584]{1,0:T(8,128)(2,1)}), bf16[1024,3584]{1,0:T(8,128)(2,1)}) %all-gather.3.cloned.1.call-update) | async-done | bytes 7340048 | tf_op jit(solution)/shard_map/all_gather | solution.py:60
  116.9 13.7 %convolution_convert_fusion.1 = bf16[512,896]{1,0:T(8,128)(2,1)} fusion(bf16[3584,896]{1,0:T(8,128)(2,1)} %param.8, bf16[1024,3584]{1,0:T(8,128)(2,1)} %all-gather.3.cloned.1.call-done, s32[512]{0:T(512)S(1)} %select_subtract_fusion), kind=kOutput, calls=%fused_computation.24 | convolution fusion | flops 7049248768 | bytes 14682112 | tf_op jit(solution)/shard_map/dot_general | solution.py:67
  130.5 18.9 %all_to_all.44 = bf16[8,64,896]{2,1,0:T(8,128)(2,1)S(1)} all-to-all(bf16[8,64,896]{2,1,0:T(8,128)(2,1)} %bitcast.134), channel_id=1, replica_groups=mesh['dp'=32,'tensor'=8] {'tensor'}, dimensions={0} | all-to-all | bytes 1835008 | tf_op jit(solution)/shard_map/all_to_all | solution.py:70
  149.6 17.7 %all_to_all.45 = bf16[8,64,896]{2,1,0:T(8,128)(2,1)} all-to-all(bf16[8,64,896]{2,1,0:T(8,128)(2,1)S(1)} %broadcast_in_dim.72), channel_id=1, replica_groups=mesh['dp'=32,'tensor'=8] {'tensor'}, dimensions={0} | all-to-all | bytes 1835008 | tf_op jit(solution)/shard_map/all_to_all | solution.py:28
  167.3 3.0 fusion.37
  170.3 33.0 %all_to_all.46 = f32[32,16,512]{2,1,0:T(8,128)S(1)} all-to-all(f32[32,16,512]{2,1,0:T(8,128)S(1)} %fusion.37), channel_id=1, replica_groups=mesh['dp'=32,'tensor'=8] {'dp'}, dimensions={0} | all-to-all | bytes 2097152 | tf_op jit(solution)/shard_map/all_to_all | solution.py:33
  204.5 7.5 %all-to-all-start.4 = ((f32[32,16,512]{2,1,0:T(8,128)}), f32[32,16,512]{2,1,0:T(8,128)S(1)}, u32[]{:S(2)}, u32[]{:S(2)}) async-start(f32[32,16,512]{2,1,0:T(8,128)} %broadcast_in_dim.73), calls=%async_computation.4 | async-start | bytes 2097152 | tf_op jit(solution)/shard_map/all_to_all | solution.py:28
  216.7 6.3 %fusion.88 = f32[1024,1024]{1,0:T(8,128)} fusion(bf16[1024,896]{1,0:T(8,128)(2,1)} %bitcast.131, bf16[1024,896]{1,0:T(8,128)(2,1)} %param.11), kind=kOutput, calls=%fused_computation.176 | convolution fusion | flops 1879048192 | bytes 7864320 | tf_op jit(solution)/shard_map/dot_general | solution.py:16
  223.0 15.5 %all-to-all-done.4 = f32[32,16,512]{2,1,0:T(8,128)S(1)} async-done(((f32[32,16,512]{2,1,0:T(8,128)}), f32[32,16,512]{2,1,0:T(8,128)S(1)}, u32[]{:S(2)}, u32[]{:S(2)}) %all-to-all-start.4) | async-done | bytes 1048608 | tf_op jit(solution)/shard_map/all_to_all | solution.py:28
  239.5 11.7 %cholesky.104 = f32[128,128]{1,0:T(8,128)S(1)} custom-call(f32[128,128]{1,0:T(8,128)S(1)} %cholesky.266), custom_call_target="Cholesky" | custom-call | tf_op jit(solution)/shard_map/jit(cholesky)/cholesky | solution.py:86
  251.4 9.8 %custom-call.32 = f32[1,128,128]{1,2,0:T(8,128)S(1)} custom-call(f32[1,128,128]{2,1,0:T(8,128)S(1)} %get-tuple-element.68), custom_call_target="InvertDiagBlocksLowerTriangular" | custom-call | tf_op jit(solution)/shard_map/jit(cholesky)/cholesky | solution.py:86
  261.9 12.1 %cholesky.217 = f32[128,128]{1,0:T(8,128)S(1)} custom-call(f32[128,128]{1,0:T(8,128)S(1)} %cholesky.270), custom_call_target="Cholesky" | custom-call | tf_op jit(solution)/shard_map/jit(cholesky)/cholesky | solution.py:86
  274.0 7.7 %all-to-all-start.5 = ((f32[32,32,1024]{2,1,0:T(8,128)}), f32[32,32,1024]{2,1,0:T(8,128)}, u32[]{:S(2)}, u32[]{:S(2)}) async-start(f32[32,32,1024]{2,1,0:T(8,128)} %bitcast.128), calls=%async_computation.5 | async-start | bytes 8388608 | tf_op jit(solution)/shard_map/all_to_all | solution.py:33
  281.7 9.8 %custom-call.33 = f32[1,128,128]{1,2,0:T(8,128)S(1)} custom-call(f32[1,128,128]{2,1,0:T(8,128)S(1)} %get-tuple-element.65), custom_call_target="InvertDiagBlocksLowerTriangular" | custom-call | tf_op jit(solution)/shard_map/jit(cholesky)/cholesky | solution.py:86
  292.2 11.7 %cholesky.238 = f32[128,128]{1,0:T(8,128)S(1)} custom-call(f32[128,128]{1,0:T(8,128)S(1)} %cholesky.275), custom_call_target="Cholesky" | custom-call | tf_op jit(solution)/shard_map/jit(cholesky)/cholesky | solution.py:86
  303.9 9.8 %custom-call.34 = f32[1,128,128]{1,2,0:T(8,128)S(1)} custom-call(f32[1,128,128]{2,1,0:T(8,128)S(1)} %get-tuple-element.62), custom_call_target="InvertDiagBlocksLowerTriangular" | custom-call | tf_op jit(solution)/shard_map/jit(cholesky)/cholesky | solution.py:86
  314.3 11.9 %cholesky.255 = f32[128,128]{1,0:T(8,128)S(1)} custom-call(f32[128,128]{1,0:T(8,128)S(1)} %convolution_subtract_fusion.6), custom_call_target="Cholesky" | custom-call | tf_op jit(solution)/shard_map/jit(cholesky)/cholesky | solution.py:86
  331.5 10.4 %while.1 = (s32[]{:T(128)}, f32[512,512]{1,0:T(8,128)S(1)}, s32[4,2]{0,1:T(2,128)S(1)}, f32[4,128,128]{2,1,0:T(8,128)}, s32[]{:T(128)}) while((s32[]{:T(128)}, f32[512,512]{1,0:T(8,128)S(1)}, s32[4,2]{0,1:T(2,128)S(1)}, f32[4,128,128]{2,1,0:T(8,128)}, s32[]{:T(128)}) %tuple.97), condition=%wide.while_cond, body=%wide.while_body.sunk | while | flops 2 | bytes 132705 | solution.py:92
  341.9 40.1 %custom-call.35 = f32[4,128,128]{1,2,0:T(8,128)S(1)} custom-call(f32[4,128,128]{2,1,0:T(8,128)} %get-tuple-element.21), custom_call_target="InvertDiagBlocksLowerTriangular" | custom-call | tf_op jit(solution)/shard_map/triangular_solve | solution.py:92
  382.7 2.9 fusion.84
  (104 shorter events, 46.3 us)
Async XLA Ops:
  7.2 109.7 %all-gather.3.cloned.1.call-start = ((), (), s32[]{:S(2)}) async-start(), calls=%async_computation.6 | async-start | bytes 7569408 | tf_op jit(solution)/shard_map/all_gather | solution.py:60
  9.0 203.3 %copy-start.4 = (pred[32]{0:T(512)(128)(4,1)}, pred[32]{0:T(512)(128)(4,1)S(1)}, u32[]{:S(2)}) copy-start(pred[32]{0:T(512)(128)(4,1)S(1)} %iota_compare_fusion.19) | copy-start | bytes 100
  12.9 11.8 %copy-start.6 = (s32[32]{0:T(128)S(1)}, s32[32]{0:T(128)}, u32[]{:S(2)}) copy-start(s32[32]{0:T(128)} %param.6) | copy-start | bytes 388
  12.9 62.5 %all-to-all-start = ((bf16[32,32,896]{2,0,1:T(8,128)(2,1)}), bf16[32,32,896]{2,0,1:T(8,128)(2,1)S(1)}, u32[]{:S(2)}, u32[]{:S(2)}) async-start(bf16[32,32,896]{2,0,1:T(8,128)(2,1)} %bitcast.127), calls=%async_computation | async-start | bytes 3670016 | tf_op jit(solution)/shard_map/all_to_all | solution.py:59
  75.4 91.9 %copy-start = (bf16[32,32,896]{2,0,1:T(8,128)(2,1)}, bf16[32,32,896]{2,0,1:T(8,128)(2,1)S(1)}, u32[]{:S(2)}) copy-start(bf16[32,32,896]{2,0,1:T(8,128)(2,1)S(1)} %all-to-all-done) | copy-start | bytes 5505028
  203.3 9.0 %copy-start.2 = (bf16[32,1024]{1,0:T(8,128)(2,1)S(1)}, bf16[32,1024]{1,0:T(8,128)(2,1)}, u32[]{:S(2)}) copy-start(bf16[32,1024]{1,0:T(8,128)(2,1)} %param.10) | copy-start | bytes 196612
  203.4 9.0 %copy-start.3 = (bf16[32,1024]{1,0:T(8,128)(2,1)S(1)}, bf16[32,1024]{1,0:T(8,128)(2,1)}, u32[]{:S(2)}) copy-start(bf16[32,1024]{1,0:T(8,128)(2,1)} %param.9) | copy-start | bytes 196612
  204.5 33.9 %all-to-all-start.4 = ((f32[32,16,512]{2,1,0:T(8,128)}), f32[32,16,512]{2,1,0:T(8,128)S(1)}, u32[]{:S(2)}, u32[]{:S(2)}) async-start(f32[32,16,512]{2,1,0:T(8,128)} %broadcast_in_dim.73), calls=%async_computation.4 | async-start | bytes 2097152 | tf_op jit(solution)/shard_map/all_to_all | solution.py:28
  212.1 119.0 %all-gather.5.cloned.1.call-start = ((), (), s32[]{:S(2)}) async-start(), calls=%async_computation.7 | async-start | bytes 2162688 | tf_op jit(solution)/shard_map/all_gather | solution.py:64
  274.0 123.9 %all-to-all-start.5 = ((f32[32,32,1024]{2,1,0:T(8,128)}), f32[32,32,1024]{2,1,0:T(8,128)}, u32[]{:S(2)}, u32[]{:S(2)}) async-start(f32[32,32,1024]{2,1,0:T(8,128)} %bitcast.128), calls=%async_computation.5 | async-start | bytes 8388608 | tf_op jit(solution)/shard_map/all_to_all | solution.py:33
  330.9 0.7 copy-start.9
  393.5 1.7 copy-start.1
  393.5 1.8 copy-start.7
  397.8 2.4 copy-start.5
  397.8 2.5 copy-start.8
Sparse Core Ops, SparseCore 0:
  11.6 105.2 all-gather.2
  216.1 81.9 all-gather.4
where the time goes:
time: 417 us; the launch traced here: 409 us
  other arithmetic  150 us (36%)
  waiting for transfers between devices  85.5 us (21%)
  blocking collectives  69.6 us (17%)
  matrix products  41.2 us (10%)
  starting transfers between devices  27.2 us (7%)
  local copies, waits for them, and re-layouts  18.3 us (4%)
  between operations  17.3 us (4%)
    another operation x14, other arithmetic, per_device(): factor = jnp.linalg.cholesky(system)  79 us
    all_gather x1, waiting for transfers between devices, per_device(): gathered = lax.all_gather(column_part, 'dp', axis=0, tiled=True)  41.5 us
    another operation x3, other arithmetic, per_device(): lax.linalg.triangular_solve(factor, middle, left_side=True, lower=True, t...  40.8 us
    all_to_all x1, blocking collectives, scatter_rows_sum(): lax.all_to_all(x.reshape((n, x.shape[0] // n) + x.shape[1:]), axis, 0, 0,...  33 us
    all_to_all x1, waiting for transfers between devices, per_device(): lax.all_to_all(masked_keys, 'dp', split_axis=1, concat_axis=0, tiled=True)  28.5 us
    all_to_all x1, blocking collectives, per_device(): lax.all_to_all(partial_q.astype(jnp.bfloat16).reshape((tensor_size, -1) +...  18.9 us
    all_to_all x1, blocking collectives, gather_rows(): lax.all_to_all(copies, axis, 0, 0, tiled=True)  17.7 us
    sub x1, other arithmetic, per_device(): row_of = owner * slot_count + compact - starts[owner]  15.8 us
  transfers between devices with their start and end apart: 5, of which 3 were waited for; matrix products, arithmetic and copies ran while one was open for 45% of the time, Pallas kernels for 0%

commit v1 on v0

--- a/solution.py
+++ b/solution.py
@@ -56,7 +56,10 @@
     own_compact = jnp.where(live_vec, starts[group_index] + slots, 0)
     masked_keys = jnp.where(live_slot, keys, jnp.zeros_like(keys))
     column_part = lax.dynamic_slice_in_dim(masked_keys, tensor_index * width_part, width_part, 1)
-    columns = lax.all_to_all(masked_keys, "dp", split_axis=1, concat_axis=0, tiled=True)
+    columns = jnp.concatenate(
+        lax.all_to_all(jnp.stack(jnp.split(masked_keys, lax.axis_size("dp"), axis=1)), "dp", 0, 0),
+        axis=0,
+    )
     gathered = lax.all_gather(column_part, "dp", axis=0, tiled=True)
     change = (targets.astype(jnp.float32) - hidden.astype(jnp.float32)) / LAYERS_LEFT
     resid_local = jnp.where(live_slot, change, jnp.zeros_like(change)).astype(jnp.bfloat16)

time: 417 us -> 424 us (1.017)
  local copies, waits for them, and re-layouts: 18.3 us -> 37 us
  waiting for transfers between devices: 85.5 us -> 73.3 us
    unnamed x20 -> x51, local copies, waits for them, and re-layouts: 0.45 us -> 19.9 us
    all_gather x1, waiting for transfers between devices: 41.5 us -> 26 us  [per_device(): gathered = lax.all_gather(column_part, 'dp', axis=0, tiled=True)]
    another operation x13 -> x14, local copies, waits for them, and re-layouts: 10.5 us -> 11.1 us
  transfers between devices with their start and end apart: 5 -> 5, of which waited for: 3 -> 3; matrix products, arithmetic and copies ran while one was open for 45% -> 48% of each run, Pallas kernels for 0% -> 0%
where the time goes in v1:
time: 424 us; the launch traced here: 416 us
  other arithmetic  150 us (35%)
  waiting for transfers between devices  73.3 us (17%)
  blocking collectives  70 us (17%)
  matrix products  41.1 us (10%)
  local copies, waits for them, and re-layouts  37 us (9%)
  starting transfers between devices  27.2 us (6%)
  between operations  17.4 us (4%)
    another operation x14, other arithmetic, per_device(): factor = jnp.linalg.cholesky(system)  79 us
    another operation x3, other arithmetic, per_device(): lax.linalg.triangular_solve(factor, middle, left_side=True, lower=True, t...  40.8 us
    all_to_all x1, blocking collectives, scatter_rows_sum(): lax.all_to_all(x.reshape((n, x.shape[0] // n) + x.shape[1:]), axis, 0, 0,...  33.4 us
    all_to_all x1, waiting for transfers between devices, per_device(): lax.all_to_all(jnp.stack(jnp.split(masked_keys, lax.axis_size('dp'), axis...  31.7 us
    all_gather x1, waiting for transfers between devices, per_device(): gathered = lax.all_gather(column_part, 'dp', axis=0, tiled=True)  26 us
    unnamed x51, local copies, waits for them, and re-layouts  19.9 us
    all_to_all x1, blocking collectives, per_device(): lax.all_to_all(partial_q.astype(jnp.bfloat16).reshape((tensor_size, -1) +...  19 us
    all_to_all x1, blocking collectives, gather_rows(): lax.all_to_all(copies, axis, 0, 0, tiled=True)  17.7 us
  transfers between devices with their start and end apart: 5, of which 3 were waited for; matrix products, arithmetic and copies ran while one was open for 48% of the time, Pallas kernels for 0%

profile of v1, /device:TPU:2, one launch (start us, length us, event | category | flops | bytes accessed | tf_op | source)
XLA Modules:
  0.0 415.5 jit_solution(13358900008816719965)
XLA Ops:
  31.5 11.8 %all-to-all-start = ((bf16[32,32,896]{2,1,0:T(8,128)(2,1)}), bf16[32,32,896]{2,1,0:T(8,128)(2,1)S(1)}, u32[]{:S(2)}, u32[]{:S(2)}) async-start(bf16[32,32,896]{2,1,0:T(8,128)(2,1)} %constant_dynamic-update-slice_fusion), calls=%async_computation | async-start | bytes 3670016 | tf_op jit(solution)/shard_map/all_to_all | solution.py:60
  45.1 4.4 %compare_select_fusion.1 = (s32[512,1]{0,1:T(1,128)S(1)}, s32[512,1]{0,1:T(1,128)S(1)}) fusion(s32[]{:T(128)} %bitcast.27, s32[]{:T(128)} %bitcast.28, s32[]{:T(128)} %bitcast.29, s32[]{:T(128)} %bitcast.30, s32[]{:T(128)} %bitcast.31, s32[]{:T(128)} %bitcast.33, s32[]{:T(128)} %bitcast.32, s32[512,1]{0,1:T(1,128)S(1)} %bitcast.256), kind=kLoop, calls=%fused_computation.199 | loop fusion | flops 7680 | bytes 6172 | tf_op jit(solution)/shard_map/gather | solution.py:49
  49.7 15.8 %select_subtract_fusion = s32[512]{0:T(512)S(1)} fusion(pred[512]{0:T(512)(128)(4,1)S(1)} %get-tuple-element.46, pred[512]{0:T(512)(128)(4,1)S(1)} %get-tuple-element.45, pred[512]{0:T(512)(128)(4,1)S(1)} %get-tuple-element.44, pred[512]{0:T(512)(128)(4,1)S(1)} %get-tuple-element.43, pred[512]{0:T(512)(128)(4,1)S(1)} %get-tuple-element.42, ...), kind=kLoop, calls=%fused_computation.208 | loop fusion | flops 14848 | bytes 19044 | tf_op jit(solution)/shard_map/sub | solution.py:49
  65.5 31.7 %all-to-all-done = bf16[32,32,896]{2,1,0:T(8,128)(2,1)S(1)} async-done(((bf16[32,32,896]{2,1,0:T(8,128)(2,1)}), bf16[32,32,896]{2,1,0:T(8,128)(2,1)S(1)}, u32[]{:S(2)}, u32[]{:S(2)}) %all-to-all-start) | async-done | bytes 1835040 | tf_op jit(solution)/shard_map/all_to_all | solution.py:60
  97.3 26.0 %all-gather.3.cloned.1.call-done = bf16[1024,3584]{1,0:T(8,128)(2,1)} async-done(((bf16[32,3584]{1,0:T(8,128)(2,1)}), bf16[1024,3584]{1,0:T(8,128)(2,1)}) %all-gather.3.cloned.1.call-update) | async-done | bytes 7340048 | tf_op jit(solution)/shard_map/all_gather | solution.py:63
  123.3 13.7 %convolution_convert_fusion.1 = bf16[512,896]{1,0:T(8,128)(2,1)} fusion(bf16[3584,896]{1,0:T(8,128)(2,1)} %param.8, bf16[1024,3584]{1,0:T(8,128)(2,1)} %all-gather.3.cloned.1.call-done, s32[512]{0:T(512)S(1)} %select_subtract_fusion), kind=kOutput, calls=%fused_computation.23 | convolution fusion | flops 7049248768 | bytes 14682112 | tf_op jit(solution)/shard_map/dot_general | solution.py:70
  137.0 19.0 %all_to_all.30 = bf16[8,64,896]{2,1,0:T(8,128)(2,1)S(1)} all-to-all(bf16[8,64,896]{2,1,0:T(8,128)(2,1)} %bitcast.254), channel_id=1, replica_groups=mesh['dp'=32,'tensor'=8] {'tensor'}, dimensions={0} | all-to-all | bytes 1835008 | tf_op jit(solution)/shard_map/all_to_all | solution.py:73
  156.2 17.7 %all_to_all.31 = bf16[8,64,896]{2,1,0:T(8,128)(2,1)} all-to-all(bf16[8,64,896]{2,1,0:T(8,128)(2,1)S(1)} %broadcast_in_dim.72), channel_id=1, replica_groups=mesh['dp'=32,'tensor'=8] {'tensor'}, dimensions={0} | all-to-all | bytes 1835008 | tf_op jit(solution)/shard_map/all_to_all | solution.py:28
  173.9 3.0 fusion.37
  176.9 33.4 %all_to_all.32 = f32[32,16,512]{2,1,0:T(8,128)S(1)} all-to-all(f32[32,16,512]{2,1,0:T(8,128)S(1)} %fusion.37), channel_id=1, replica_groups=mesh['dp'=32,'tensor'=8] {'dp'}, dimensions={0} | all-to-all | bytes 2097152 | tf_op jit(solution)/shard_map/all_to_all | solution.py:33
  211.5 7.5 %all-to-all-start.4 = ((f32[32,16,512]{2,1,0:T(8,128)}), f32[32,16,512]{2,1,0:T(8,128)S(1)}, u32[]{:S(2)}, u32[]{:S(2)}) async-start(f32[32,16,512]{2,1,0:T(8,128)} %broadcast_in_dim.73), calls=%async_computation.4 | async-start | bytes 2097152 | tf_op jit(solution)/shard_map/all_to_all | solution.py:28
  223.6 6.3 %fusion.88 = f32[1024,1024]{1,0:T(8,128)} fusion(bf16[1024,896]{1,0:T(8,128)(2,1)} %bitcast.251, bf16[1024,896]{1,0:T(8,128)(2,1)} %param.11), kind=kOutput, calls=%fused_computation.239 | convolution fusion | flops 1879048192 | bytes 7864320 | tf_op jit(solution)/shard_map/dot_general | solution.py:16
  229.9 15.5 %all-to-all-done.4 = f32[32,16,512]{2,1,0:T(8,128)S(1)} async-done(((f32[32,16,512]{2,1,0:T(8,128)}), f32[32,16,512]{2,1,0:T(8,128)S(1)}, u32[]{:S(2)}, u32[]{:S(2)}) %all-to-all-start.4) | async-done | bytes 1048608 | tf_op jit(solution)/shard_map/all_to_all | solution.py:28
  246.4 11.7 %cholesky.104 = f32[128,128]{1,0:T(8,128)S(1)} custom-call(f32[128,128]{1,0:T(8,128)S(1)} %cholesky.266), custom_call_target="Cholesky" | custom-call | tf_op jit(solution)/shard_map/jit(cholesky)/cholesky | solution.py:89
  258.3 9.8 %custom-call.32 = f32[1,128,128]{1,2,0:T(8,128)S(1)} custom-call(f32[1,128,128]{2,1,0:T(8,128)S(1)} %get-tuple-element.68), custom_call_target="InvertDiagBlocksLowerTriangular" | custom-call | tf_op jit(solution)/shard_map/jit(cholesky)/cholesky | solution.py:89
  268.8 12.1 %cholesky.217 = f32[128,128]{1,0:T(8,128)S(1)} custom-call(f32[128,128]{1,0:T(8,128)S(1)} %cholesky.270), custom_call_target="Cholesky" | custom-call | tf_op jit(solution)/shard_map/jit(cholesky)/cholesky | solution.py:89
  280.9 7.6 %all-to-all-start.5 = ((f32[32,32,1024]{2,1,0:T(8,128)}), f32[32,32,1024]{2,1,0:T(8,128)}, u32[]{:S(2)}, u32[]{:S(2)}) async-start(f32[32,32,1024]{2,1,0:T(8,128)} %bitcast.248), calls=%async_computation.5 | async-start | bytes 8388608 | tf_op jit(solution)/shard_map/all_to_all | solution.py:33
  288.6 9.8 %custom-call.33 = f32[1,128,128]{1,2,0:T(8,128)S(1)} custom-call(f32[1,128,128]{2,1,0:T(8,128)S(1)} %get-tuple-element.65), custom_call_target="InvertDiagBlocksLowerTriangular" | custom-call | tf_op jit(solution)/shard_map/jit(cholesky)/cholesky | solution.py:89
  299.1 11.7 %cholesky.238 = f32[128,128]{1,0:T(8,128)S(1)} custom-call(f32[128,128]{1,0:T(8,128)S(1)} %cholesky.275), custom_call_target="Cholesky" | custom-call | tf_op jit(solution)/shard_map/jit(cholesky)/cholesky | solution.py:89
  310.8 9.8 %custom-call.34 = f32[1,128,128]{1,2,0:T(8,128)S(1)} custom-call(f32[1,128,128]{2,1,0:T(8,128)S(1)} %get-tuple-element.62), custom_call_target="InvertDiagBlocksLowerTriangular" | custom-call | tf_op jit(solution)/shard_map/jit(cholesky)/cholesky | solution.py:89
  321.2 11.9 %cholesky.255 = f32[128,128]{1,0:T(8,128)S(1)} custom-call(f32[128,128]{1,0:T(8,128)S(1)} %convolution_subtract_fusion.6), custom_call_target="Cholesky" | custom-call | tf_op jit(solution)/shard_map/jit(cholesky)/cholesky | solution.py:89
  338.4 10.4 %while.1 = (s32[]{:T(128)}, f32[512,512]{1,0:T(8,128)S(1)}, s32[4,2]{0,1:T(2,128)S(1)}, f32[4,128,128]{2,1,0:T(8,128)}, s32[]{:T(128)}) while((s32[]{:T(128)}, f32[512,512]{1,0:T(8,128)S(1)}, s32[4,2]{0,1:T(2,128)S(1)}, f32[4,128,128]{2,1,0:T(8,128)}, s32[]{:T(128)}) %tuple.97), condition=%wide.while_cond, body=%wide.while_body.sunk | while | flops 2 | bytes 132205 | solution.py:95
  348.8 40.1 %custom-call.35 = f32[4,128,128]{1,2,0:T(8,128)S(1)} custom-call(f32[4,128,128]{2,1,0:T(8,128)} %get-tuple-element.21), custom_call_target="InvertDiagBlocksLowerTriangular" | custom-call | tf_op jit(solution)/shard_map/triangular_solve | solution.py:95
  389.6 2.9 fusion.84
  (135 shorter events, 64.9 us)
Async XLA Ops:
  7.2 116.2 %all-gather.3.cloned.1.call-start = ((), (), s32[]{:S(2)}) async-start(), calls=%async_computation.6 | async-start | bytes 7569408 | tf_op jit(solution)/shard_map/all_gather | solution.py:63
  9.0 210.2 %copy-start.4 = (pred[32]{0:T(512)(128)(4,1)}, pred[32]{0:T(512)(128)(4,1)S(1)}, u32[]{:S(2)}) copy-start(pred[32]{0:T(512)(128)(4,1)S(1)} %iota_compare_fusion.19) | copy-start | bytes 100
  31.5 11.8 %copy-start.6 = (s32[32]{0:T(128)S(1)}, s32[32]{0:T(128)}, u32[]{:S(2)}) copy-start(s32[32]{0:T(128)} %param.6) | copy-start | bytes 388
  31.5 65.7 %all-to-all-start = ((bf16[32,32,896]{2,1,0:T(8,128)(2,1)}), bf16[32,32,896]{2,1,0:T(8,128)(2,1)S(1)}, u32[]{:S(2)}, u32[]{:S(2)}) async-start(bf16[32,32,896]{2,1,0:T(8,128)(2,1)} %constant_dynamic-update-slice_fusion), calls=%async_computation | async-start | bytes 3670016 | tf_op jit(solution)/shard_map/all_to_all | solution.py:60
  97.3 76.6 %copy-start = (bf16[32,32,896]{2,1,0:T(8,128)(2,1)}, bf16[32,32,896]{2,1,0:T(8,128)(2,1)S(1)}, u32[]{:S(2)}) copy-start(bf16[32,32,896]{2,1,0:T(8,128)(2,1)S(1)} %all-to-all-done) | copy-start | bytes 5505028
  210.3 8.9 %copy-start.2 = (bf16[32,1024]{1,0:T(8,128)(2,1)S(1)}, bf16[32,1024]{1,0:T(8,128)(2,1)}, u32[]{:S(2)}) copy-start(bf16[32,1024]{1,0:T(8,128)(2,1)} %param.10) | copy-start | bytes 196612
  210.3 8.9 %copy-start.3 = (bf16[32,1024]{1,0:T(8,128)(2,1)S(1)}, bf16[32,1024]{1,0:T(8,128)(2,1)}, u32[]{:S(2)}) copy-start(bf16[32,1024]{1,0:T(8,128)(2,1)} %param.9) | copy-start | bytes 196612
  211.5 33.9 %all-to-all-start.4 = ((f32[32,16,512]{2,1,0:T(8,128)}), f32[32,16,512]{2,1,0:T(8,128)S(1)}, u32[]{:S(2)}, u32[]{:S(2)}) async-start(f32[32,16,512]{2,1,0:T(8,128)} %broadcast_in_dim.73), calls=%async_computation.4 | async-start | bytes 2097152 | tf_op jit(solution)/shard_map/all_to_all | solution.py:28
  219.0 118.9 %all-gather.5.cloned.1.call-start = ((), (), s32[]{:S(2)}) async-start(), calls=%async_computation.7 | async-start | bytes 2162688 | tf_op jit(solution)/shard_map/all_gather | solution.py:67
  280.9 123.8 %all-to-all-start.5 = ((f32[32,32,1024]{2,1,0:T(8,128)}), f32[32,32,1024]{2,1,0:T(8,128)}, u32[]{:S(2)}, u32[]{:S(2)}) async-start(f32[32,32,1024]{2,1,0:T(8,128)} %bitcast.248), calls=%async_computation.5 | async-start | bytes 8388608 | tf_op jit(solution)/shard_map/all_to_all | solution.py:33
  337.8 0.7 copy-start.9
  400.4 1.7 copy-start.1
  400.4 1.8 copy-start.7
  404.7 2.4 copy-start.5
  404.7 2.5 copy-start.8
Sparse Core Ops, SparseCore 0:
  11.6 111.6 all-gather.2
  223.0 82.1 all-gather.4
